TPU v7x, 32 devices: a whole 2x2x4 slice. The times are simulated.
32 devices in a mesh: dp: 4 (over z), expert: 8 (over y, x, core).
Axes of the slice: x: 2, y: 2, z: 4, core: 2. Of those that a mesh axis runs over, the one named last changes fastest.
Arguments:
- hidden: bfloat16 [3072, 2880], P('expert', 'dp'), may hold values from -6 to 6
- segments: int32 [8, 384], P('expert'), may hold values from 0 to 3, never falling along the last dimension, each value on 1 to 192 neighbouring positions
- request_adapter: int32 [8, 4], P('expert'), may hold values from 0 to 7
- routes: int32 [8, 384, 4], P('expert', 'dp'), may hold values from 0 to 7, all different within a row; in each aligned block of 96 rows (0 to 95, 96 to 191, ..., all dimensions but the last counted through in order) at most 64 rows name the same one
- expert_gates: bfloat16 [8, 384, 4], P('expert', 'dp'), may hold values from 0.049804688 to 0.59765625
- attention_gain: float32 [2880], replicated, may hold values from 0.25 to 1.75
- joined_weight: bfloat16 [2880, 4, 640], P(None, 'dp'), may hold values from -0.109375 to 0.109375
- sinks: float32 [32], P('dp'), may hold values from 0 to 3
- attention_out_weight: bfloat16 [2048, 2880], P('dp'), may hold values from -0.125 to 0.125
- joined_down_maps: bfloat16 [2880, 128], replicated, may hold values from -0.109375 to 0.109375
- joined_up_maps: bfloat16 [128, 4, 640], P(None, 'dp'), may hold values from -0.375 to 0.375
- output_down_maps: bfloat16 [2048, 128], P('dp'), may hold values from -0.125 to 0.125
- output_up_maps: bfloat16 [128, 2880], P(None, 'dp'), may hold values from -0.75 to 0.75
- expert_norm_gain: float32 [2880], replicated, may hold values from 0.25 to 1.75
- expert_gate_weight: bfloat16 [8, 2880, 2880], P('expert', None, 'dp'), may hold values from -0.109375 to 0.109375
- expert_up_weight: bfloat16 [8, 2880, 2880], P('expert', None, 'dp'), may hold values from -0.109375 to 0.109375
- expert_down_weight: bfloat16 [8, 2880, 2880], P('expert', 'dp'), may hold values from -0.109375 to 0.109375
- closing_gain: float32 [2880], replicated, may hold values from 0.25 to 1.75
- vocabulary_weight: bfloat16 [2880, 25600], P(None, ('dp', 'expert')), may hold values from -0.109375 to 0.109375
Outputs:
- hidden_out: bfloat16 [3072, 2880], P('expert', 'dp')
- logits: float32 [32, 25600], P(None, ('dp', 'expert'))
Inputs may be any that keep to these rules, and one draw needn't show every extreme that they name: `segments`: in each column the ids do not fall; each of the 4 requests has 1 to 192 tokens, and one has exactly 192. `routes`: the 4 experts of a token differ. Within the rows of one device (96 consecutive tokens, aligned blocks) no expert is named more than 64 times, and in some blocks one expert is named exactly 64 times.
All inputs are finite; a program needn't handle non-finite values.
Results may differ from a plain program's by a relative error of at most 0.02.
Values may be sent and summed in bfloat16 or wider, within the bound.
No kernel may reach another device: no remote copies, remote signals or barrier semaphores. Data moves between devices by JAX's collectives and lax.ppermute only.
A program may use at most 128 MiB of HBM per device.

v0:
```python
import jax
import jax.numpy as jnp
from jax import lax
from jax.sharding import PartitionSpec as P

HEAD_SIZE = 64
QUERY_GROUP = 8
TOP = 4
ADAPTER_RANK = 16
REQS = 4
epsilon = 1e-05
theta_base = 150000.0
adapter_scale = 2.0
glu_alpha = 1.702


def rms_scale(values, gain_row):
    mean_square = jnp.mean(values * values, axis=-1, keepdims=True)
    return values * lax.rsqrt(mean_square + epsilon) * gain_row


def positions_of(segment_row):
    counter = jnp.arange(segment_row.shape[0], dtype=jnp.int32)
    starting = jnp.concatenate(
        [jnp.ones((1,), dtype=jnp.bool_), segment_row[1:] != segment_row[:-1]]
    )
    first_index = lax.cummax(jnp.where(starting, counter, 0), axis=0)
    return counter - first_index


def adapter_per_token(segment_row, adapter_row):
    hits = segment_row[:, None] == jnp.arange(adapter_row.shape[0], dtype=jnp.int32)[None, :]
    return jnp.sum(jnp.where(hits, adapter_row[None, :], 0), axis=1)


def rotate_heads(values, positions):
    head_dim = values.shape[-1]
    half_dim = head_dim // 2
    frequency = theta_base ** (-2.0 * jnp.arange(half_dim, dtype=jnp.float32) / head_dim)
    angles = positions.astype(jnp.float32)[:, None] * frequency[None, :]
    cosine = jnp.cos(angles)[:, None, :]
    sine_part = jnp.sin(angles)[:, None, :]
    first_half = values[..., :half_dim]
    second_half = values[..., half_dim:]
    return jnp.concatenate(
        [
            first_half * cosine - second_half * sine_part,
            second_half * cosine + first_half * sine_part,
        ],
        axis=-1,
    )


def attend_heads(queries, key_heads, value_heads, segment_row, sink_row):
    tokens_now, kv_now, group_now, head_dim = queries.shape
    scores = jnp.einsum(
        "tkgh,skh->kgts", queries, key_heads, preferred_element_type=jnp.float32
    ) * head_dim ** (-0.5)
    counter = jnp.arange(tokens_now, dtype=jnp.int32)
    allowed = (segment_row[:, None] == segment_row[None, :]) & (
        counter[None, :] <= counter[:, None]
    )
    weights = jnp.where(allowed[None, None], jnp.exp(scores), 0.0)
    totals = jnp.sum(weights, axis=-1, keepdims=True) + jnp.exp(sink_row).reshape(
        kv_now, group_now, 1, 1
    )
    probs = (weights / totals).astype(jnp.bfloat16)
    blended_hidden = jnp.einsum(
        "kgts,skh->tkgh", probs, value_heads, preferred_element_type=jnp.float32
    )
    return blended_hidden.astype(jnp.bfloat16).reshape(tokens_now, kv_now * group_now * head_dim)


def shards(
    hidden,
    segments,
    request_adapter,
    routes,
    expert_gates,
    attention_gain,
    joined_weight,
    sinks,
    attention_out_weight,
    joined_down_maps,
    joined_up_maps,
    output_down_maps,
    output_up_maps,
    expert_norm_gain,
    expert_gate_weight,
    expert_up_weight,
    expert_down_weight,
    closing_gain,
    vocabulary_weight,
):
    groups = lax.axis_size("dp")
    columns = lax.axis_size("expert")
    position_dp = lax.axis_index("dp")
    segment_row = segments[0]
    adapter_row = request_adapter[0]
    col_tokens = segment_row.shape[0]
    gathered_rows = lax.all_gather(hidden, "dp", axis=1, tiled=True)
    width = gathered_rows.shape[1]
    normalized_hidden = rms_scale(gathered_rows.astype(jnp.float32), attention_gain).astype(
        jnp.bfloat16
    )
    joined_projection = jnp.dot(
        normalized_hidden, joined_weight.reshape(width, -1), preferred_element_type=jnp.float32
    )
    reduced_every_adapter = joined_down_maps.shape[1]
    reduced_hidden = jnp.dot(
        normalized_hidden, joined_down_maps, preferred_element_type=jnp.float32
    ).astype(jnp.bfloat16)
    rank_owner = jnp.arange(reduced_every_adapter, dtype=jnp.int32) // ADAPTER_RANK
    adapter_mask = adapter_per_token(segment_row, adapter_row)[:, None] == rank_owner[None, :]
    selected_reduced = jnp.where(adapter_mask, reduced_hidden, jnp.zeros_like(reduced_hidden))
    joined_projection = joined_projection + adapter_scale * jnp.dot(
        selected_reduced,
        joined_up_maps.reshape(reduced_every_adapter, -1),
        preferred_element_type=jnp.float32,
    )
    kv_here = joined_weight.shape[1]
    joined_projection = joined_projection.reshape(col_tokens, kv_here, QUERY_GROUP + 2, HEAD_SIZE)
    positions = positions_of(segment_row)
    queries = rotate_heads(
        joined_projection[:, :, :QUERY_GROUP].reshape(col_tokens, kv_here * QUERY_GROUP, HEAD_SIZE),
        positions,
    )
    queries = queries.astype(jnp.bfloat16).reshape(col_tokens, kv_here, QUERY_GROUP, HEAD_SIZE)
    key_heads = rotate_heads(joined_projection[:, :, QUERY_GROUP], positions).astype(jnp.bfloat16)
    value_heads = joined_projection[:, :, QUERY_GROUP + 1].astype(jnp.bfloat16)
    blended_hidden = attend_heads(queries, key_heads, value_heads, segment_row, sinks)
    partial_out = jnp.dot(blended_hidden, attention_out_weight, preferred_element_type=jnp.float32)
    mine_out = lax.psum_scatter(
        partial_out.astype(jnp.bfloat16), "dp", scatter_dimension=1, tiled=True
    ).astype(jnp.float32)
    output_reduced = lax.psum(
        jnp.dot(blended_hidden, output_down_maps, preferred_element_type=jnp.float32).astype(
            jnp.bfloat16
        ),
        "dp",
    )
    selected_output = jnp.where(adapter_mask, output_reduced, jnp.zeros_like(output_reduced))
    adapter_delta = adapter_scale * jnp.dot(
        selected_output, output_up_maps, preferred_element_type=jnp.float32
    )
    resid = (hidden.astype(jnp.float32) + mine_out + adapter_delta).astype(jnp.bfloat16)
    share = col_tokens // groups
    column_full = lax.all_gather(resid, "dp", axis=1, tiled=True)
    own_rows = lax.dynamic_slice_in_dim(column_full, position_dp * share, share, 0)
    moe_in = rms_scale(
        lax.optimization_barrier(own_rows).astype(jnp.float32), expert_norm_gain
    ).astype(jnp.bfloat16)
    experts = expert_gate_weight.shape[0] * columns
    capacity = 4 * share * TOP // (3 * experts)
    route_flat = routes[0].reshape(-1)
    one_hot = (route_flat[:, None] == jnp.arange(experts, dtype=jnp.int32)[None, :]).astype(
        jnp.int32
    )
    slot_rows = jnp.sum((jnp.cumsum(one_hot, axis=0) - one_hot) * one_hot, axis=1)
    target = route_flat * capacity + slot_rows
    source_rows = jnp.arange(route_flat.shape[0], dtype=jnp.int32) // TOP
    table = jnp.full((experts * capacity,), share, jnp.int32).at[target].set(source_rows)
    padded = jnp.concatenate([moe_in, jnp.zeros((1, width), jnp.bfloat16)], axis=0)
    outgoing = jnp.take(padded, table, axis=0).reshape(experts, capacity, width)
    gate_weight = expert_gate_weight[0]
    up_weight = expert_up_weight[0]
    down_weight = expert_down_weight[0]
    copies = jnp.tile(outgoing, (groups, 1, 1))
    arrived = lax.all_to_all(copies, ("dp", "expert"), split_axis=0, concat_axis=0, tiled=True)
    senders = arrived.shape[0]
    slots_now = arrived.shape[1]
    rows_in = arrived.reshape(-1, width)
    gate_part = jnp.dot(rows_in, gate_weight, preferred_element_type=jnp.float32)
    up_part = jnp.dot(rows_in, up_weight, preferred_element_type=jnp.float32)
    activated = (gate_part * jax.nn.sigmoid(glu_alpha * gate_part) * (up_part + 1.0)).astype(
        jnp.bfloat16
    )
    shares_out = (
        jnp.dot(activated, down_weight, preferred_element_type=jnp.float32)
        .astype(jnp.bfloat16)
        .reshape(senders, slots_now, width)
    )
    answers = lax.all_to_all(shares_out, ("dp", "expert"), split_axis=0, concat_axis=0, tiled=True)
    merged = jnp.sum(
        answers.reshape(groups, columns, capacity, width).astype(jnp.float32), axis=0
    ).astype(jnp.bfloat16)
    picked_out = jnp.take(merged.reshape(experts * capacity, width), target, axis=0).reshape(
        share, TOP, width
    )
    mixture = jnp.einsum(
        "tk,tkd->td", expert_gates[0], picked_out, preferred_element_type=jnp.float32
    )
    moe_rounded = lax.optimization_barrier(mixture.astype(jnp.bfloat16))
    finished = (own_rows.astype(jnp.float32) + moe_rounded.astype(jnp.float32)).astype(jnp.bfloat16)
    hidden_out = lax.all_to_all(finished, "dp", split_axis=1, concat_axis=0, tiled=True)
    counter = jnp.arange(col_tokens, dtype=jnp.int32)
    request_ids = jnp.arange(REQS, dtype=jnp.int32)
    last_index = jnp.max(
        jnp.where(segment_row[None, :] == request_ids[:, None], counter[None, :], -1), axis=1
    )
    local_index = last_index - position_dp * share
    inside = (local_index >= 0) & (local_index < share)
    chosen = jnp.take(finished, jnp.clip(local_index, 0, share - 1), axis=0)
    chosen = jnp.where(inside[:, None], chosen, jnp.zeros_like(chosen))
    ends = rms_scale(chosen.astype(jnp.float32), closing_gain).astype(jnp.bfloat16)
    spread_rows = lax.all_gather(ends, ("dp", "expert"), axis=0, tiled=True)
    tail_rows = jnp.sum(
        spread_rows.reshape(groups, columns * REQS, width).astype(jnp.float32), axis=0
    ).astype(jnp.bfloat16)
    logits = jnp.dot(tail_rows, vocabulary_weight, preferred_element_type=jnp.float32)
    return (hidden_out, logits)


def solution(mesh):
    in_specs = (
        P("expert", "dp"),
        P("expert", None),
        P("expert", None),
        P("expert", "dp", None),
        P("expert", "dp", None),
        P(),
        P(None, "dp", None),
        P("dp"),
        P("dp", None),
        P(),
        P(None, "dp", None),
        P("dp", None),
        P(None, "dp"),
        P(),
        P("expert", None, "dp"),
        P("expert", None, "dp"),
        P("expert", "dp", None),
        P(),
        P(None, ("dp", "expert")),
    )
    out_specs = (P("expert", "dp"), P(None, ("dp", "expert")))
    return jax.shard_map(shards, mesh=mesh, in_specs=in_specs, out_specs=out_specs, check_vma=False)
```

profile of v0, /device:TPU:0, one launch (start us, length us, event | category | flops | bytes accessed | tf_op | source)
XLA Modules:
  0.0 916.7 jit_solution(5084641404369946867)
XLA Ops:
  12.1 48.3 %all-gather.4.cloned.1.call-done = bf16[384,2880]{0,1:T(8,128)(2,1)} async-done(((bf16[384,720]{0,1:T(8,128)(2,1)}), bf16[384,2880]{0,1:T(8,128)(2,1)}) %all-gather.4.cloned.1.call-update) | async-done | bytes 2211856 | tf_op jit(solution)/shard_map/all_gather | solution.py:101
  60.4 2.2 fusion
  62.6 5.9 fusion.11
  68.5 4.8 fusion.21
  73.3 2.5 copy.59
  79.6 2.2 fusion.23
  83.7 4.1 convolution_convert_fusion.1
  87.9 29.0 %all-reduce.3.cloned.1.call-done = bf16[384,128]{1,0:T(8,128)(2,1)} async-done(((bf16[384,128]{1,0:T(8,128)(2,1)}), bf16[384,128]{1,0:T(8,128)(2,1)}) %all-reduce.3.cloned.1.call-update) | async-done | bytes 98320 | tf_op jit(solution)/shard_map/psum | solution.py:136
  116.8 48.0 %reduce-scatter.2.cloned.1.call-done = bf16[384,720]{0,1:T(8,128)(2,1)} async-done(((bf16[384,2880]{0,1:T(8,128)(2,1)}), bf16[384,720]{0,1:T(8,128)(2,1)}) %reduce-scatter.2.cloned.1.call-update) | async-done | bytes 552976 | tf_op jit(solution)/shard_map/reduce_scatter | solution.py:133
  164.9 2.4 fusion.22
  169.2 3.1 scatter_custom_fusion
  172.4 42.6 %all-gather.6.cloned.1.call-done = bf16[384,2880]{0,1:T(8,128)(2,1)} async-done(((bf16[384,720]{0,1:T(8,128)(2,1)}), bf16[384,2880]{0,1:T(8,128)(2,1)}) %all-gather.6.cloned.1.call-update) | async-done | bytes 2211856 | tf_op jit(solution)/shard_map/all_gather | solution.py:148
  215.0 1.7 constant_dynamic-slice_fusion
  217.9 3.7 gather_fusion
  221.6 2.2 broadcast_select_fusion
  223.8 6.0 tile.8
  229.8 266.5 %all_to_all.29 = bf16[32,64,2880]{2,1,0:T(8,128)(2,1)} all-to-all(bf16[32,64,2880]{2,1,0:T(8,128)(2,1)} %bitcast.115), channel_id=1, replica_groups=mesh['dp'=4,'expert'=8] {'dp','expert'}, dimensions={0} | all-to-all | bytes 23592960 | tf_op jit(solution)/shard_map/all_to_all | solution.py:169
  496.3 15.1 %fusion.4 = f32[2048,720]{0,1:T(8,128)} fusion(bf16[2048,2880]{1,0:T(8,128)(2,1)} %bitcast.26, bf16[1,2880,720]{1,2,0:T(8,128)(2,1)} %param.34), kind=kOutput, calls=%fused_computation.15 | convolution fusion | flops 8493465600 | bytes 21841920 | tf_op jit(solution)/shard_map/dot_general | solution.py:174
  511.4 26.6 %convolution_convert_fusion = bf16[2048,2880]{0,1:T(8,128)(2,1)} fusion(bf16[1,720,2880]{2,1,0:T(8,128)(2,1)} %param.35, f32[2048,720]{0,1:T(8,128)} %fusion.4, bf16[2048,2880]{1,0:T(8,128)(2,1)} %bitcast.26, bf16[1,2880,720]{1,2,0:T(8,128)(2,1)} %param.33), kind=kOutput, calls=%fused_computation.4 | convolution fusion | flops 17004625920 | bytes 37785600 | tf_op jit(solution)/shard_map/dot_general | solution.py:179
  538.0 16.3 %copy.67 = bf16[2048,2880]{1,0:T(8,128)(2,1)} copy(bf16[2048,2880]{0,1:T(8,128)(2,1)} %convolution_convert_fusion) | data formatting | bytes 23592960 | tf_op jit(solution)/shard_map/convert_element_type | solution.py:180
  554.4 4.1 all-to-all-start.1
  559.1 266.6 %all-to-all-done.1 = bf16[32,64,2880]{2,1,0:T(8,128)(2,1)} async-done(((bf16[32,64,2880]{2,1,0:T(8,128)(2,1)}), bf16[32,64,2880]{2,1,0:T(8,128)(2,1)}, u32[]{:S(2)}, u32[]{:S(2)}) %all-to-all-start.1) | async-done | bytes 11796512 | tf_op jit(solution)/shard_map/all_to_all | solution.py:183
  825.7 6.8 reduce_sum.89
  832.5 3.5 gather_fusion.1
  836.0 2.6 gather.19
  838.6 4.7 multiply_reduce_fusion
  843.6 1.7 add_convert_fusion
  847.6 3.5 all-to-all-start.2
  851.2 49.2 %all-gather = bf16[32,4,2880]{2,1,0:T(4,128)(2,1)} all-gather(bf16[1,4,2880]{2,1,0:T(4,128)(2,1)S(1)} %fusion.60), channel_id=1, replica_groups=mesh['dp'=4,'expert'=8] {'dp','expert'}, dimensions={0}, use_global_device_ids=true | all-gather | bytes 760320 | tf_op jit(solution)/shard_map/all_gather | solution.py:206
  900.4 2.3 reshape.444
  902.7 2.0 reduce_sum.91
  904.6 4.5 fusion.79
  (94 shorter events, 18.0 us)
Async XLA Ops:
  7.2 76.5 %copy-start = (bf16[512,2880]{0,1:T(8,128)(2,1)S(1)}, bf16[512,2880]{0,1:T(8,128)(2,1)}, u32[]{:S(2)}) copy-start(bf16[512,2880]{0,1:T(8,128)(2,1)} %param.27) | copy-start | bytes 8847364
  7.2 53.2 %all-gather.4.cloned.1.call-start = ((), (), s32[]{:S(2)}) async-start(), calls=%async_computation.4 | async-start | bytes 2764800 | tf_op jit(solution)/shard_map/all_gather | solution.py:101
  7.9 108.9 %all-reduce.3.cloned.1.call-start = ((), (), s32[]{:S(2)}) async-start(), calls=%async_computation.6 | async-start | bytes 196608 | tf_op jit(solution)/shard_map/psum | solution.py:136
  62.6 6.0 copy-start.9
  62.6 6.0 copy-start.10
  79.6 3.0 copy-start.4
  81.9 0.8 copy-start.3
  83.6 81.3 %copy-start.2 = (bf16[384,720]{0,1:T(8,128)(2,1)S(1)}, bf16[384,720]{0,1:T(8,128)(2,1)}, u32[]{:S(2)}) copy-start(bf16[384,720]{0,1:T(8,128)(2,1)} %param.19) | copy-start | bytes 1658884
  83.6 81.3 %reduce-scatter.2.cloned.1.call-start = ((), (), s32[]{:S(2)}) async-start(), calls=%async_computation.5 | async-start | bytes 2764800 | tf_op jit(solution)/shard_map/reduce_scatter | solution.py:133
  87.8 79.6 %copy-start.5 = (s32[1,96,4]{1,2,0:T(4,128)S(1)}, s32[1,96,4]{1,2,0:T(4,128)}, u32[]{:S(2)}) copy-start(s32[1,96,4]{1,2,0:T(4,128)} %param.22) | copy-start | bytes 4612
  87.8 129.3 %copy-start.6 = (f32[2880]{0:T(1024)S(1)}, f32[2880]{0:T(1024)}, u32[]{:S(2)}) copy-start(f32[2880]{0:T(1024)} %param.32) | copy-start | bytes 34564
  87.8 127.2 %all-gather.6.cloned.1.call-start = ((), (), s32[]{:S(2)}) async-start(), calls=%async_computation.7 | async-start | bytes 2764800 | tf_op jit(solution)/shard_map/all_gather | solution.py:148
  554.4 4.4 copy-start.8
  554.4 271.3 %all-to-all-start.1 = ((bf16[32,64,2880]{2,1,0:T(8,128)(2,1)}), bf16[32,64,2880]{2,1,0:T(8,128)(2,1)}, u32[]{:S(2)}, u32[]{:S(2)}) async-start(bf16[32,64,2880]{2,1,0:T(8,128)(2,1)} %bitcast.114), calls=%async_computation.2 | async-start | bytes 24117248 | tf_op jit(solution)/shard_map/all_to_all | solution.py:183
  843.2 7.8 copy-start.7
  847.6 61.5 %all-to-all-start.2 = ((bf16[96,4,720]{2,0,1:T(8,128)(2,1)}), bf16[96,4,720]{2,0,1:T(8,128)(2,1)S(1)}, u32[]{:S(2)}, u32[]{:S(2)}) async-start(bf16[96,4,720]{2,0,1:T(8,128)(2,1)} %copy.68), calls=%async_computation.3 | async-start | bytes 1179648 | tf_op jit(solution)/shard_map/all_to_all | solution.py:195
  851.2 59.0 %copy-start.1 = (bf16[512,2880]{0,1:T(8,128)(2,1)S(1)}, bf16[512,2880]{0,1:T(8,128)(2,1)}, u32[]{:S(2)}) copy-start(bf16[512,2880]{0,1:T(8,128)(2,1)} %param.27) | copy-start | bytes 8847364
Sparse Core Ops, SparseCore 0:
  9.6 50.7 all-gather.3
  83.7 33.0 all-reduce.2
  119.3 45.5 reduce-scatter.1
  167.5 47.4 all-gather.5
where the time goes:
time: 918 us; the launch traced here: 917 us
  waiting for transfers between devices  435 us (47%)
  blocking collectives  316 us (34%)
  matrix products  68 us (7%)
  local copies, waits for them, and re-layouts  50.3 us (5%)
  other arithmetic  25.7 us (3%)
  between operations  14.1 us (2%)
    all_to_all x1, waiting for transfers between devices, shards(): lax.all_to_all(shares_out, ('dp', 'expert'), split_axis=0, concat_axis=0,...  267 us
    all_to_all x1, blocking collectives, shards(): lax.all_to_all(copies, ('dp', 'expert'), split_axis=0, concat_axis=0, til...  266 us
    all_gather x1, blocking collectives, shards(): spread_rows = lax.all_gather(ends, ('dp', 'expert'), axis=0, tiled=True)  49.2 us
    all_gather x1, waiting for transfers between devices, shards(): gathered_rows = lax.all_gather(hidden, 'dp', axis=1, tiled=True)  48.3 us
    reduce_scatter x1, waiting for transfers between devices, shards(): lax.psum_scatter(partial_out.astype(jnp.bfloat16), 'dp', scatter_dimensio...  48 us
    all_gather x1, waiting for transfers between devices, shards(): column_full = lax.all_gather(resid, 'dp', axis=1, tiled=True)  42.6 us
    psum x1, waiting for transfers between devices, shards(): lax.psum(jnp.dot(blended_hidden, output_down_maps, preferred_element_type...  29 us
    dot_general x1, matrix products, shards(): jnp.dot(activated, down_weight, preferred_element_type=jnp.float32)  26.6 us
  transfers between devices with their start and end apart: 6, of which 5 were waited for; matrix products, arithmetic and copies ran while one was open for 2% of the time, Pallas kernels for 0%

commit v1 on v0

--- a/solution.py
+++ b/solution.py
@@ -145,7 +145,18 @@
     )
     resid = (hidden.astype(jnp.float32) + mine_out + adapter_delta).astype(jnp.bfloat16)
     share = col_tokens // groups
-    column_full = lax.all_gather(resid, "dp", axis=1, tiled=True)
+    then = jax.lax.axis_size("dp")
+    before = jax.lax.axis_index("dp")
+    v1, far_arr, fresh = (then, before, resid.shape[1])
+    wide_out, front = (resid, 1)
+    while front < v1:
+        entries = []
+        for q in [*range(v1)]:
+            entries.append((q, (q - front) % v1))
+        value_now = jax.lax.ppermute(wide_out, "dp", entries)
+        wide_out = jnp.concatenate([wide_out, value_now], 1)
+        front = 2 * front
+    column_full = jnp.roll(wide_out, far_arr * fresh, 1)
     own_rows = lax.dynamic_slice_in_dim(column_full, position_dp * share, share, 0)
     moe_in = rms_scale(
         lax.optimization_barrier(own_rows).astype(jnp.float32), expert_norm_gain

time: 918 us -> 956 us (1.041)
  starting transfers between devices: 7.73 us -> 20.7 us
  waiting for transfers between devices: 435 us -> 447 us
    ppermute x0 -> x2, waiting for transfers between devices: none -> 54.6 us  [shards(): value_now = jax.lax.ppermute(wide_out, 'dp', entries)]
    all_gather x1 -> x0, waiting for transfers between devices: 42.6 us -> none  [shards(): column_full = lax.all_gather(resid, 'dp', axis=1, tiled=True)]
    ppermute x0 -> x2, starting transfers between devices: none -> 13 us  [shards(): value_now = jax.lax.ppermute(wide_out, 'dp', entries)]
  transfers between devices with their start and end apart: 6 -> 7, of which waited for: 5 -> 6; matrix products, arithmetic and copies ran while one was open for 2% -> 2% of each run, Pallas kernels for 0% -> 0%
where the time goes in v1:
time: 956 us; the launch traced here: 947 us
  waiting for transfers between devices  447 us (47%)
  blocking collectives  317 us (33%)
  matrix products  66.8 us (7%)
  local copies, waits for them, and re-layouts  55.2 us (6%)
  other arithmetic  26 us (3%)
  starting transfers between devices  20.7 us (2%)
  between operations  14.5 us (2%)
    all_to_all x1, blocking collectives, shards(): lax.all_to_all(copies, ('dp', 'expert'), split_axis=0, concat_axis=0, til...  268 us
    all_to_all x1, waiting for transfers between devices, shards(): lax.all_to_all(shares_out, ('dp', 'expert'), split_axis=0, concat_axis=0,...  267 us
    ppermute x2, waiting for transfers between devices, shards(): value_now = jax.lax.ppermute(wide_out, 'dp', entries)  54.6 us
    all_gather x1, blocking collectives, shards(): spread_rows = lax.all_gather(ends, ('dp', 'expert'), axis=0, tiled=True)  49.2 us
    all_gather x1, waiting for transfers between devices, shards(): gathered_rows = lax.all_gather(hidden, 'dp', axis=1, tiled=True)  48.3 us
    reduce_scatter x1, waiting for transfers between devices, shards(): lax.psum_scatter(partial_out.astype(jnp.bfloat16), 'dp', scatter_dimensio...  48 us
    psum x1, waiting for transfers between devices, shards(): lax.psum(jnp.dot(blended_hidden, output_down_maps, preferred_element_type...  29 us
    dot_general x1, matrix products, shards(): jnp.dot(activated, down_weight, preferred_element_type=jnp.float32)  26.6 us
  transfers between devices with their start and end apart: 7, of which 6 were waited for; matrix products, arithmetic and copies ran while one was open for 2% of the time, Pallas kernels for 0%

profile of v1, /device:TPU:0, one launch (start us, length us, event | category | flops | bytes accessed | tf_op | source)
XLA Modules:
  0.0 947.4 jit_solution(6750126829561829352)
XLA Ops:
  12.1 48.3 %all-gather.3.cloned.1.call-done = bf16[384,2880]{0,1:T(8,128)(2,1)} async-done(((bf16[384,720]{0,1:T(8,128)(2,1)}), bf16[384,2880]{0,1:T(8,128)(2,1)}) %all-gather.3.cloned.1.call-update) | async-done | bytes 2211856 | tf_op jit(solution)/shard_map/all_gather | solution.py:101
  60.4 2.2 fusion
  62.6 5.9 fusion.11
  68.5 4.8 fusion.21
  73.3 2.5 copy.59
  79.6 2.2 fusion.23
  83.7 4.1 convolution_convert_fusion.1
  87.8 29.0 %all-reduce.3.cloned.1.call-done = bf16[384,128]{1,0:T(8,128)(2,1)} async-done(((bf16[384,128]{1,0:T(8,128)(2,1)}), bf16[384,128]{1,0:T(8,128)(2,1)}) %all-reduce.3.cloned.1.call-update) | async-done | bytes 98320 | tf_op jit(solution)/shard_map/psum | solution.py:136
  116.9 48.0 %reduce-scatter.2.cloned.1.call-done = bf16[384,720]{0,1:T(8,128)(2,1)} async-done(((bf16[384,2880]{0,1:T(8,128)(2,1)}), bf16[384,720]{0,1:T(8,128)(2,1)}) %reduce-scatter.2.cloned.1.call-update) | async-done | bytes 552976 | tf_op jit(solution)/shard_map/reduce_scatter | solution.py:133
  164.9 2.5 constant_dynamic-update-slice_fusion.5
  167.4 10.9 %collective-permute-start = (bf16[384,720]{0,1:T(8,128)(2,1)S(1)}, bf16[384,720]{0,1:T(8,128)(2,1)S(1)}, u32[]{:S(2)}, u32[]{:S(2)}) collective-permute-start(bf16[384,720]{0,1:T(8,128)(2,1)S(1)} %get-tuple-element.23), channel_id=1, source_target_pairs={{0,24},{8,0},{16,8},{24,16},{1,25},{9,1},{17,9},{25,17},{2,26},{10... | collective-permute-start | bytes 1658888 | tf_op jit(solution)/shard_map/ppermute | solution.py:156
  179.6 11.4 %collective-permute-done = bf16[384,720]{0,1:T(8,128)(2,1)S(1)} collective-permute-done((bf16[384,720]{0,1:T(8,128)(2,1)S(1)}, bf16[384,720]{0,1:T(8,128)(2,1)S(1)}, u32[]{:S(2)}, u32[]{:S(2)}) %collective-permute-start) | collective-permute-done | bytes 552992 | tf_op jit(solution)/shard_map/ppermute | solution.py:156
  191.1 2.1 collective-permute-start.1
  193.8 2.9 scatter_custom_fusion
  197.7 43.2 %collective-permute-done.1 = bf16[384,1440]{0,1:T(8,128)(2,1)S(1)} collective-permute-done((bf16[384,1440]{0,1:T(8,128)(2,1)S(1)}, bf16[384,1440]{0,1:T(8,128)(2,1)S(1)}, u32[]{:S(2)}, u32[]{:S(2)}) %collective-permute-start.1) | collective-permute-done | bytes 1105952 | tf_op jit(solution)/shard_map/ppermute | solution.py:156
  247.9 3.7 gather_fusion
  251.6 2.2 broadcast_select_fusion
  253.9 6.0 tile.8
  259.9 267.9 %all_to_all.29 = bf16[32,64,2880]{2,1,0:T(8,128)(2,1)} all-to-all(bf16[32,64,2880]{2,1,0:T(8,128)(2,1)} %bitcast.115), channel_id=1, replica_groups=mesh['dp'=4,'expert'=8] {'dp','expert'}, dimensions={0} | all-to-all | bytes 23592960 | tf_op jit(solution)/shard_map/all_to_all | solution.py:180
  527.8 13.9 %fusion.4 = f32[2048,720]{0,1:T(8,128)} fusion(bf16[2048,2880]{1,0:T(8,128)(2,1)} %bitcast.26, bf16[1,2880,720]{1,2,0:T(8,128)(2,1)S(1)} %bitcast.127), kind=kOutput, calls=%fused_computation.15 | convolution fusion | flops 8493465600 | bytes 21841920 | tf_op jit(solution)/shard_map/dot_general | solution.py:185
  541.6 26.6 %convolution_convert_fusion = bf16[2048,2880]{0,1:T(8,128)(2,1)} fusion(bf16[1,720,2880]{2,1,0:T(8,128)(2,1)} %param.35, f32[2048,720]{0,1:T(8,128)} %fusion.4, bf16[2048,2880]{1,0:T(8,128)(2,1)} %bitcast.26, bf16[1,2880,720]{1,2,0:T(8,128)(2,1)} %param.33), kind=kOutput, calls=%fused_computation.4 | convolution fusion | flops 17004625920 | bytes 37785600 | tf_op jit(solution)/shard_map/dot_general | solution.py:190
  568.3 16.3 %copy.67 = bf16[2048,2880]{1,0:T(8,128)(2,1)} copy(bf16[2048,2880]{0,1:T(8,128)(2,1)} %convolution_convert_fusion) | data formatting | bytes 23592960 | tf_op jit(solution)/shard_map/convert_element_type | solution.py:191
  584.6 4.1 all-to-all-start.1
  589.3 266.6 %all-to-all-done.1 = bf16[32,64,2880]{2,1,0:T(8,128)(2,1)} async-done(((bf16[32,64,2880]{2,1,0:T(8,128)(2,1)}), bf16[32,64,2880]{2,1,0:T(8,128)(2,1)}, u32[]{:S(2)}, u32[]{:S(2)}) %all-to-all-start.1) | async-done | bytes 11796512 | tf_op jit(solution)/shard_map/all_to_all | solution.py:194
  855.9 6.8 reduce_sum.89
  862.7 3.5 gather_fusion.1
  866.2 2.6 gather.19
  868.8 4.7 multiply_reduce_fusion
  878.0 3.5 all-to-all-start.2
  881.5 49.2 %all-gather = bf16[32,4,2880]{2,1,0:T(4,128)(2,1)} all-gather(bf16[1,4,2880]{2,1,0:T(4,128)(2,1)S(1)} %fusion.60), channel_id=1, replica_groups=mesh['dp'=4,'expert'=8] {'dp','expert'}, dimensions={0}, use_global_device_ids=true | all-gather | bytes 760320 | tf_op jit(solution)/shard_map/all_gather | solution.py:217
  930.7 2.3 reshape.444
  935.0 4.5 fusion.79
  (105 shorter events, 28.6 us)
Async XLA Ops:
  7.2 76.5 %copy-start = (bf16[512,2880]{0,1:T(8,128)(2,1)S(1)}, bf16[512,2880]{0,1:T(8,128)(2,1)}, u32[]{:S(2)}) copy-start(bf16[512,2880]{0,1:T(8,128)(2,1)} %param.27) | copy-start | bytes 8847364
  7.2 53.2 %all-gather.3.cloned.1.call-start = ((), (), s32[]{:S(2)}) async-start(), calls=%async_computation.4 | async-start | bytes 2764800 | tf_op jit(solution)/shard_map/all_gather | solution.py:101
  7.9 109.0 %all-reduce.3.cloned.1.call-start = ((), (), s32[]{:S(2)}) async-start(), calls=%async_computation.6 | async-start | bytes 196608 | tf_op jit(solution)/shard_map/psum | solution.py:136
  62.6 6.0 copy-start.9
  62.6 6.0 copy-start.10
  79.6 3.0 copy-start.4
  81.9 0.8 copy-start.3
  83.6 81.3 %copy-start.2 = (bf16[384,720]{0,1:T(8,128)(2,1)S(1)}, bf16[384,720]{0,1:T(8,128)(2,1)}, u32[]{:S(2)}) copy-start(bf16[384,720]{0,1:T(8,128)(2,1)} %param.19) | copy-start | bytes 1658884
  83.6 81.3 %reduce-scatter.2.cloned.1.call-start = ((), (), s32[]{:S(2)}) async-start(), calls=%async_computation.5 | async-start | bytes 2764800 | tf_op jit(solution)/shard_map/reduce_scatter | solution.py:133
  87.8 90.5 %copy-start.5 = (s32[1,96,4]{1,2,0:T(4,128)S(1)}, s32[1,96,4]{1,2,0:T(4,128)}, u32[]{:S(2)}) copy-start(s32[1,96,4]{1,2,0:T(4,128)} %param.22) | copy-start | bytes 4612
  167.4 23.6 %collective-permute-start = (bf16[384,720]{0,1:T(8,128)(2,1)S(1)}, bf16[384,720]{0,1:T(8,128)(2,1)S(1)}, u32[]{:S(2)}, u32[]{:S(2)}) collective-permute-start(bf16[384,720]{0,1:T(8,128)(2,1)S(1)} %get-tuple-element.23), channel_id=1, source_target_pairs={{0,24},{8,0},{16,8},{24,16},{1,25},{9,1},{17,9},{25,17},{2,26},{10... | collective-permute-start | bytes 1658888 | tf_op jit(solution)/shard_map/ppermute | solution.py:156
  191.1 49.7 %collective-permute-start.1 = (bf16[384,1440]{0,1:T(8,128)(2,1)S(1)}, bf16[384,1440]{0,1:T(8,128)(2,1)S(1)}, u32[]{:S(2)}, u32[]{:S(2)}) collective-permute-start(bf16[384,1440]{0,1:T(8,128)(2,1)S(1)} %pad_maximum_fusion), channel_id=1, source_target_pairs={{0,16},{8,24},{16,0},{24,8},{1,17},{9,25},{17,1},{25,9},{2,18},{10... | collective-permute-start | bytes 3317768 | tf_op jit(solution)/shard_map/ppermute | solution.py:156
  197.7 49.4 %copy-start.6 = (f32[2880]{0:T(1024)S(1)}, f32[2880]{0:T(1024)}, u32[]{:S(2)}) copy-start(f32[2880]{0:T(1024)} %param.32) | copy-start | bytes 34564
  253.9 273.9 %slice-start = ((s8[4239360]{0:T(1024)(128)(4,1)}), s8[45056]{0:T(1024)(128)(4,1)S(1)}, s32[]{:S(2)}) async-start(s8[4239360]{0:T(1024)(128)(4,1)} %bitcast.126), calls=%async_computation.7 | async-start | bytes 90112
  259.9 267.9 %slice-start.1 = ((s8[4239360]{0:T(1024)(128)(4,1)}), s8[4194304]{0:T(1024)(128)(4,1)S(1)}, s32[]{:S(2)}) async-start(s8[4239360]{0:T(1024)(128)(4,1)} %bitcast.126), calls=%async_computation.8 | async-start | bytes 8388608
  584.6 4.4 copy-start.8
  584.6 271.3 %all-to-all-start.1 = ((bf16[32,64,2880]{2,1,0:T(8,128)(2,1)}), bf16[32,64,2880]{2,1,0:T(8,128)(2,1)}, u32[]{:S(2)}, u32[]{:S(2)}) async-start(bf16[32,64,2880]{2,1,0:T(8,128)(2,1)} %bitcast.114), calls=%async_computation.2 | async-start | bytes 24117248 | tf_op jit(solution)/shard_map/all_to_all | solution.py:194
  873.4 8.0 copy-start.7
  878.0 61.5 %all-to-all-start.2 = ((bf16[96,4,720]{2,0,1:T(8,128)(2,1)}), bf16[96,4,720]{2,0,1:T(8,128)(2,1)S(1)}, u32[]{:S(2)}, u32[]{:S(2)}) async-start(bf16[96,4,720]{2,0,1:T(8,128)(2,1)} %copy.68), calls=%async_computation.3 | async-start | bytes 1179648 | tf_op jit(solution)/shard_map/all_to_all | solution.py:206
  881.5 59.0 %copy-start.1 = (bf16[512,2880]{0,1:T(8,128)(2,1)S(1)}, bf16[512,2880]{0,1:T(8,128)(2,1)}, u32[]{:S(2)}) copy-start(bf16[512,2880]{0,1:T(8,128)(2,1)} %param.27) | copy-start | bytes 8847364
Sparse Core Ops, SparseCore 0:
  9.6 50.7 all-gather.2
  83.7 33.1 all-reduce.2
  119.3 45.5 reduce-scatter.1
